TPU v7x, 256 devices: a whole 4x4x8 slice. The times are simulated.
256 devices in a mesh: snap: 4 (over x), line: 64 (over z, y, core).
Axes of the slice: x: 4, y: 4, z: 8, core: 2. Of those that a mesh axis runs over, the one named last changes fastest.
Arguments:
- ptdf_rows: float32 [8192, 20480], P('line'), may hold values from -4 to 4
- plan: float32 [5120, 2048], P(('snap', 'line')), may hold values from 0 to 0.15
- unit_bus: int32 [5120], replicated, may hold values from 0 to 20479
- min_up: int32 [5120], P(('snap', 'line')), may hold values from 1 to 24, as said below
- ramp_lag: int32 [5120], P(('snap', 'line')), may hold values from 1 to 6, as said below
- load_share: float32 [20480], replicated, may hold values from 0.004 to 0.04
- system_load: float32 [2048], P('snap'), may hold values from 0.6 to 1.4
- corridor_order: int32 [4], replicated, may hold values from 0 to 3, each once
- corridor_buses: int32 [4, 2], replicated, may hold values from 0 to 20479, as said below
- corridor_owner: int32 [4], replicated, may hold values from 0 to 63
- corridor_row: int32 [4], replicated, may hold values from 0 to 127
- corridor_ratio: float32 [4], replicated, may hold values from 0.5 to 2
Outputs:
- flows: float32 [8192, 2048], P('line', 'snap')
- corridor_sens: float32 [4, 20480], replicated
Inputs may be any that keep to these rules, and one draw needn't show every extreme that they name: `min_up`: some unit has a window of exactly 24. `ramp_lag`: some unit has a lag of exactly 6. `corridor_buses`: the two buses of a corridor differ.
All inputs are finite; a program needn't handle non-finite values.
Results may differ from a plain program's by a relative error of at most 0.000098.
Values sent between devices are 32-bit elements; how exact they have to be, the bound alone decides.
No kernel may reach another device: no remote copies, remote signals or barrier semaphores. Data moves between devices by JAX's collectives and lax.ppermute only.
A program may use at most 128 MiB of HBM per device.

v0:
```python
import jax
import jax.numpy as jnp
from jax import lax
from jax.sharding import Mesh
from jax.sharding import PartitionSpec as P

WMAX = 24
NC = 4
LINE = ("line_0", "line_1", "line_2")
SNAP_LINE = ("snap", "line_0", "line_1", "line_2")
ramp_gain = 0.5


def body(
    ptdf_rows,
    plan,
    unit_bus,
    min_up,
    ramp_lag,
    load_share,
    system_load,
    corridor_order,
    corridor_buses,
    corridor_owner,
    corridor_row,
    corridor_ratio,
):
    unit_count, horizon = plan.shape
    snap_count = lax.axis_size("snap")
    line_count = lax.axis_size(LINE)
    here = lax.axis_index(LINE)
    picked_rows = []
    for step in range(NC):
        chosen = corridor_order[step]
        row = lax.dynamic_index_in_dim(ptdf_rows, corridor_row[chosen], 0, keepdims=False)
        picked_rows.append(jnp.where(corridor_owner[chosen] == here, row, 0.0))
    all_rows = lax.psum(jnp.stack(picked_rows), LINE)
    padded = jnp.pad(plan, ((0, 0), (WMAX, 0)))
    inverse = 1.0 / min_up.astype(jnp.float32)
    held_mean = jnp.zeros(plan.shape, jnp.float32)
    lagged = jnp.zeros(plan.shape, jnp.float32)
    for offset in range(WMAX):
        shifted = padded[:, WMAX - offset : WMAX - offset + horizon]
        held_mean = held_mean + shifted * jnp.where(offset < min_up, inverse, 0.0)[:, None]
        lagged = lagged + shifted * (ramp_lag == offset).astype(jnp.float32)[:, None]
    dispatch = held_mean + ramp_gain * (plan - lagged)
    unit_blocks = lax.all_to_all(dispatch, "snap", split_axis=1, concat_axis=0, tiled=True)
    everyone = lax.all_gather(unit_blocks, LINE, axis=0, tiled=True)
    order_ids = unit_bus.reshape(snap_count, line_count, unit_count).transpose(1, 0, 2).reshape(-1)
    columns = jnp.concatenate(
        [jnp.take(ptdf_rows, order_ids, axis=1), jnp.take(all_rows, order_ids, axis=1)], axis=0
    )
    load_flows = jnp.dot(
        ptdf_rows, load_share, preferred_element_type=jnp.float32, precision=lax.Precision.HIGHEST
    )
    row_load_flows = jnp.dot(
        all_rows, load_share, preferred_element_type=jnp.float32, precision=lax.Precision.HIGHEST
    )
    sens_list = []
    weights = []
    row_coeff_list = []
    ends_list = []
    for step in range(NC):
        chosen = corridor_order[step]
        bus_from = corridor_buses[chosen, 0]
        bus_to = corridor_buses[chosen, 1]
        ratio = corridor_ratio[chosen]
        initial = all_rows[step]
        row_coeffs = []
        for prior in range(step):
            prior_from, prior_to = ends_list[prior]
            value = initial[prior_from] - initial[prior_to]
            for earlier in range(prior):
                value = value - row_coeffs[earlier] * (
                    sens_list[earlier][prior_from] - sens_list[earlier][prior_to]
                )
            row_coeffs.append(value)
        current = initial
        for prior in range(step):
            current = current - row_coeffs[prior] * sens_list[prior]
        weight = ratio / (1.0 + ratio * jnp.abs(current[bus_from] - current[bus_to]))
        sens_list.append(weight * current)
        weights.append(weight)
        row_coeff_list.append(row_coeffs)
        ends_list.append((bus_from, bus_to))
    coeff_list = []
    for step in range(NC):
        bus_from, bus_to = ends_list[step]
        coefficient = ptdf_rows[:, bus_from] - ptdf_rows[:, bus_to]
        for prior in range(step):
            coefficient = coefficient - coeff_list[prior] * (
                sens_list[prior][bus_from] - sens_list[prior][bus_to]
            )
        coeff_list.append(coefficient)
    flows_all = jnp.dot(
        columns, everyone, preferred_element_type=jnp.float32, precision=lax.Precision.HIGHEST
    )
    lines_here = ptdf_rows.shape[0]
    base = flows_all[:lines_here] - load_flows[:, None] * system_load[None, :]
    row_base = flows_all[lines_here:] - row_load_flows[:, None] * system_load[None, :]
    shift_list = []
    for step in range(NC):
        line_flow = row_base[step]
        for prior in range(step):
            line_flow = line_flow - row_coeff_list[step][prior] * shift_list[prior]
        shift_list.append(weights[step] * line_flow)
    flows = base
    for step in range(NC):
        flows = flows - coeff_list[step][:, None] * shift_list[step][None, :]
    return (flows, jnp.stack(sens_list))


def solution(mesh):
    torus = Mesh(
        mesh.devices.reshape(mesh.shape["snap"], 8, 4, 2), ("snap", "line_0", "line_1", "line_2")
    )
    in_specs = (
        P(LINE, None),
        P(SNAP_LINE, None),
        P(),
        P(SNAP_LINE),
        P(SNAP_LINE),
        P(),
        P("snap"),
        P(),
        P(),
        P(),
        P(),
        P(),
    )
    out_specs = (P(LINE, "snap"), P())
    return jax.shard_map(body, mesh=torus, in_specs=in_specs, out_specs=out_specs, check_vma=False)
```

profile of v0, /device:TPU:1, one launch (start us, length us, event | category | flops | bytes accessed | tf_op | source)
XLA Modules:
  0.0 346.1 jit_solution(17711845217591911878)
XLA Ops:
  7.2 0.0 copy-start
  7.2 0.7 compare_convert_fusion.23
  7.9 0.7 compare_select_fusion.25
  8.6 0.7 compare_select_fusion.24
  9.3 6.7 %multiply_add_fusion = f32[20,2048]{1,0:T(8,128)S(1)} fusion(f32[20,2048]{1,0:T(8,128)} %param.13, f32[20]{0:T(128)S(1)} %get-tuple-element.133, f32[20]{0:T(128)S(1)} %get-tuple-element.134, f32[20]{0:T(128)S(1)} %get-tuple-element.112, f32[20]{0:T(128)S(1)} %get-tuple-element.113, f32[20]{0:T(128)S(1)} %get-tuple-element.114, ...), kind=kLoop, calls=%fused_computation.17 | loop fusion | flops 3973120 | bytes 331520 | tf_op jit(solution)/shard_map/add | solution.py:46
  16.0 0.1 all_to_all.14
  16.1 0.7 copy.43
  16.8 4.8 %all-to-all-start = ((f32[20,4,512]{2,0,1:T(8,128)}), f32[20,4,512]{2,0,1:T(8,128)S(1)}, u32[]{:S(2)}, u32[]{:S(2)}) async-start(f32[20,4,512]{2,0,1:T(8,128)} %copy.43), calls=%async_computation | async-start | bytes 393216 | tf_op jit(solution)/shard_map/all_to_all | solution.py:47
  21.7 0.0 all-reduce.3.cloned.1.call-start
  21.7 1.5 fusion.22
  30.9 1.5 fusion.20
  42.7 2.0 broadcast_select_fusion.3
  44.7 1.0 pad_maximum_fusion
  45.7 0.0 all-reduce.3.cloned.1.call-update
  45.8 0.2 all-gather.2.cloned.1.call-start
  46.0 0.9 reshape.180
  46.9 0.1 copy.39
  47.0 0.2 reshape.182
  47.2 0.2 reshape.181
  47.3 11.8 %copy.41 = f32[128,20480]{0,1:T(8,128)} copy(f32[128,20480]{1,0:T(8,128)} %param.12) | data formatting | bytes 20971520 | tf_op args[0]
  59.1 21.6 %gather_fusion = f32[5120,128]{1,0:T(8,128)} fusion(f32[128,20480]{0,1:T(8,128)} %copy.41, s32[5120]{0:T(1024)S(1)} %broadcast_clamp_fusion), kind=kCustom, calls=%fused_computation | custom fusion | bytes 5263360 | tf_op jit(solution)/shard_map/jit(_take)/gather | solution.py:51
  80.8 4.2 %select_bitcast_fusion.1 = f32[128,5120]{0,1:T(8,128)S(1)} fusion(f32[5120,128]{1,0:T(8,128)} %gather_fusion, pred[5120]{0:T(1024)(128)(4,1)S(1)} %compare_and_fusion), kind=kLoop, calls=%fused_computation.7 | loop fusion | flops 655360 | bytes 5248000 | tf_op jit(solution)/shard_map/jit(_take)/select_n | solution.py:51
  85.0 0.0 copy-done
  85.0 0.0 copy-start.2
  85.0 0.0 copy-start.4
  85.0 10.8 %convolution_bitcast_fusion.1 = f32[128]{0:T(128)S(1)} fusion(f32[128,20480]{1,0:T(8,128)} %param.12, f32[20480,1]{0,1:T(1,128)S(1)} %bitcast.62), kind=kOutput, calls=%fused_computation.9 | convolution fusion | flops 31457280 | bytes 10568192 | tf_op jit(solution)/shard_map/dot_general | solution.py:53
  95.9 0.0 copy-done.2
  95.9 0.7 constant_dynamic-slice_fusion.36
  111.9 0.0 copy-done.4
  111.9 0.7 fusion.19
  112.6 0.0 all-to-all-done
  112.6 0.7 all_to_all.17
  113.3 0.0 all-gather.2.cloned.1.call-update
  113.3 116.0 %all-reduce.3.cloned.1.call-done = f32[4,20480]{1,0:T(4,128)} async-done(((f32[4,20480]{1,0:T(4,128)}), f32[4,20480]{1,0:T(4,128)}) %all-reduce.3.cloned.1.call-update) | async-done | bytes 327696 | tf_op jit(solution)/shard_map/psum | solution.py:37
  229.3 0.0 copy-start.1
  229.4 6.5 %copy.42 = f32[4,20480]{0,1:T(8,128)} copy(f32[4,20480]{1,0:T(4,128)} %all-reduce.3.cloned.1.call-done) | data formatting | bytes 655360 | tf_op jit(solution)/shard_map/psum | solution.py:37
  235.9 21.6 %gather_fusion.1 = f32[5120,4]{1,0:T(8,128)} fusion(f32[4,20480]{0,1:T(8,128)} %copy.42, s32[5120]{0:T(1024)S(1)} %broadcast_clamp_fusion), kind=kCustom, calls=%fused_computation.1 | custom fusion | bytes 184320 | tf_op jit(solution)/shard_map/jit(_take)/gather | solution.py:51
  257.5 0.0 copy-done.1
  257.5 0.1 fusion.18
  257.6 0.7 constant_dynamic-slice_fusion.26
  258.3 0.6 constant_dynamic-slice_fusion.32
  262.8 0.2 multiply_subtract_fusion.2
  263.0 0.7 constant_dynamic-slice_fusion.24
  266.1 0.7 constant_dynamic-slice_fusion.16
  269.3 0.7 constant_dynamic-slice_fusion.10
  271.2 0.2 multiply_subtract_fusion.1
  271.5 0.7 constant_dynamic-slice_fusion.4
  274.7 0.7 constant_dynamic-slice_fusion
  280.2 0.7 constant_dynamic-slice_fusion.8
  282.2 0.2 multiply_subtract_fusion
  282.4 0.7 constant_dynamic-slice_fusion.12
  285.7 0.7 constant_dynamic-slice_fusion.30
  290.2 1.1 multiply_subtract_fusion.4
  291.3 1.2 fusion.8
  292.5 1.5 convolution_bitcast_fusion
  294.0 5.4 %select_bitcast_fusion = f32[4,5120]{0,1:T(8,128)} fusion(f32[5120,4]{1,0:T(8,128)} %gather_fusion.1, pred[5120]{0:T(1024)(128)(4,1)S(1)} %compare_and_fusion), kind=kLoop, calls=%fused_computation.6 | loop fusion | flops 20480 | bytes 168960 | tf_op jit(solution)/shard_map/jit(_take)/select_n | solution.py:51
  299.4 0.1 broadcast_multiply_fusion.1
  299.5 1.0 pad_maximum_fusion.1
  300.5 0.0 copy-start.3
  300.5 17.4 %all-gather.2.cloned.1.call-done = f32[5120,512]{1,0:T(8,128)} async-done(((f32[80,512]{1,0:T(8,128)}), f32[5120,512]{1,0:T(8,128)}) %all-gather.2.cloned.1.call-update) | async-done | bytes 10485776 | tf_op jit(solution)/shard_map/all_gather | solution.py:48
  317.9 20.4 %fusion = f32[132,512]{1,0:T(8,128)S(1)} fusion(f32[5120,512]{1,0:T(8,128)} %all-gather.2.cloned.1.call-done, f32[4,5120]{0,1:T(8,128)} %select_bitcast_fusion, f32[128,5120]{0,1:T(8,128)S(1)} %select_bitcast_fusion.1), kind=kOutput, calls=%fused_computation.2 | convolution fusion | flops 4153036800 | bytes 13459456 | tf_op jit(solution)/shard_map/dot_general | solution.py:95
  338.3 0.0 copy-done.3
  338.3 0.1 slice_subtract_fusion.1
  338.4 0.9 fusion.7
  (4 shorter events, 0.1 us)
Async XLA Ops:
  7.2 77.9 %copy-start = (f32[20480]{0:T(1024)S(1)}, f32[20480]{0:T(1024)}, u32[]{:S(2)}) copy-start(f32[20480]{0:T(1024)} %param.17) | copy-start | bytes 245764
  16.8 95.8 %all-to-all-start = ((f32[20,4,512]{2,0,1:T(8,128)}), f32[20,4,512]{2,0,1:T(8,128)S(1)}, u32[]{:S(2)}, u32[]{:S(2)}) async-start(f32[20,4,512]{2,0,1:T(8,128)} %copy.43), calls=%async_computation | async-start | bytes 393216 | tf_op jit(solution)/shard_map/all_to_all | solution.py:47
  21.7 207.7 %all-reduce.3.cloned.1.call-start = ((), (), s32[]{:S(2)}) async-start(), calls=%async_computation.1 | async-start | bytes 655360 | tf_op jit(solution)/shard_map/psum | solution.py:37
  45.8 272.2 %all-gather.2.cloned.1.call-start = ((), (), s32[]{:S(2)}) async-start(), calls=%async_computation.2 | async-start | bytes 10649600 | tf_op jit(solution)/shard_map/all_gather | solution.py:48
  85.0 10.8 %copy-start.2 = (s32[4,2]{0,1:T(2,128)S(1)}, s32[4,2]{0,1:T(2,128)}, u32[]{:S(2)}) copy-start(s32[4,2]{0,1:T(2,128)} %param.20) | copy-start | bytes 100
  85.0 26.9 %copy-start.4 = (f32[4]{0:T(128)S(1)}, f32[4]{0:T(128)}, u32[]{:S(2)}) copy-start(f32[4]{0:T(128)} %param.23) | copy-start | bytes 52
  229.3 28.2 %copy-start.1 = (f32[4,20480]{1,0:T(4,128)S(1)}, f32[4,20480]{1,0:T(4,128)}, u32[]{:S(2)}) copy-start(f32[4,20480]{1,0:T(4,128)} %all-reduce.3.cloned.1.call-done) | copy-start | bytes 983044
  300.5 37.8 %copy-start.3 = (f32[512]{0:T(512)S(1)}, f32[512]{0:T(512)}, u32[]{:S(2)}) copy-start(f32[512]{0:T(512)} %param.18) | copy-start | bytes 6148
Sparse Core Ops, SparseCore 0:
  45.9 183.4 all-reduce.2
  232.7 85.2 all-gather.1
where the time goes:
time: 348 us; the launch traced here: 346 us
  waiting for transfers between devices  133 us (38%)
  local copies, waits for them, and re-layouts  75.6 us (22%)
  between operations  72.9 us (21%)
  matrix products  32.7 us (9%)
  other arithmetic  26.4 us (8%)
  starting transfers between devices  5.06 us (1%)
    psum x1, waiting for transfers between devices, body(): all_rows = lax.psum(jnp.stack(picked_rows), LINE)  116 us
    gather x1, local copies, waits for them, and re-layouts, body(): jnp.take(ptdf_rows, order_ids, axis=1)  21.6 us
    gather x1, local copies, waits for them, and re-layouts, body(): jnp.take(all_rows, order_ids, axis=1)  21.6 us
    dot_general x1, matrix products, body(): jnp.dot(columns, everyone, preferred_element_type=jnp.float32, precision=...  20.4 us
    all_gather x1, waiting for transfers between devices, body(): everyone = lax.all_gather(unit_blocks, LINE, axis=0, tiled=True)  17.4 us
    unnamed x11, local copies, waits for them, and re-layouts  11.8 us
    dot_general x1, matrix products, body(): jnp.dot(ptdf_rows, load_share, preferred_element_type=jnp.float32, precis...  10.8 us
  transfers between devices with their start and end apart: 3, of which 2 were waited for; matrix products, arithmetic and copies ran while one was open for 30% of the time, Pallas kernels for 0%

commit v1 on v0

--- a/solution.py
+++ b/solution.py
@@ -9,6 +9,10 @@
 LINE = ("line_0", "line_1", "line_2")
 SNAP_LINE = ("snap", "line_0", "line_1", "line_2")
 ramp_gain = 0.5
+
+
+def form_row(piece_in, device_axis):
+    return jnp.sum(lax.all_gather(piece_in, axis_name=device_axis), 0)
 
 
 def body(
@@ -34,7 +38,7 @@
         chosen = corridor_order[step]
         row = lax.dynamic_index_in_dim(ptdf_rows, corridor_row[chosen], 0, keepdims=False)
         picked_rows.append(jnp.where(corridor_owner[chosen] == here, row, 0.0))
-    all_rows = lax.psum(jnp.stack(picked_rows), LINE)
+    all_rows = form_row(jnp.stack(picked_rows), LINE)
     padded = jnp.pad(plan, ((0, 0), (WMAX, 0)))
     inverse = 1.0 / min_up.astype(jnp.float32)
     held_mean = jnp.zeros(plan.shape, jnp.float32)

time: 348 us -> 266 us (0.76)
  waiting for transfers between devices: 133 us -> 43.8 us
  other arithmetic: 26.4 us -> 36.4 us
    psum x1 -> x0, waiting for transfers between devices: 116 us -> none  [body(): all_rows = lax.psum(jnp.stack(picked_rows), LINE)]
    all_gather x0 -> x1, waiting for transfers between devices: none -> 33.6 us  [form_row(): return jnp.sum(lax.all_gather(piece_in, axis_name=device_axis), 0)]
    reduce_sum x0 -> x1, other arithmetic: none -> 10.8 us  [form_row(): return jnp.sum(lax.all_gather(piece_in, axis_name=device_axis), 0)]
    all_gather x1, waiting for transfers between devices: 17.4 us -> 10.1 us  [body(): everyone = lax.all_gather(unit_blocks, LINE, axis=0, tiled=True)]
    psum x1 -> x0, local copies, waits for them, and re-layouts: 6.55 us -> none  [body(): all_rows = lax.psum(jnp.stack(picked_rows), LINE)]
    reduce_sum x0 -> x1, local copies, waits for them, and re-layouts: none -> 5.56 us  [form_row(): return jnp.sum(lax.all_gather(piece_in, axis_name=device_axis), 0)]
    unnamed x11 -> x9, local copies, waits for them, and re-layouts: 11.8 us -> 11.9 us
  transfers between devices with their start and end apart: 3 -> 3, of which waited for: 2 -> 2; matrix products, arithmetic and copies ran while one was open for 30% -> 43% of each run, Pallas kernels for 0% -> 0%
where the time goes in v1:
time: 266 us; the launch traced here: 265 us
  local copies, waits for them, and re-layouts  74.8 us (28%)
  between operations  72.1 us (27%)
  waiting for transfers between devices  43.8 us (16%)
  other arithmetic  36.4 us (14%)
  matrix products  32.7 us (12%)
  starting transfers between devices  4.87 us (2%)
    all_gather x1, waiting for transfers between devices, form_row(): return jnp.sum(lax.all_gather(piece_in, axis_name=device_axis), 0)  33.6 us
    gather x1, local copies, waits for them, and re-layouts, body(): jnp.take(ptdf_rows, order_ids, axis=1)  21.9 us
    gather x1, local copies, waits for them, and re-layouts, body(): jnp.take(all_rows, order_ids, axis=1)  21.7 us
    dot_general x1, matrix products, body(): jnp.dot(columns, everyone, preferred_element_type=jnp.float32, precision=...  20.4 us
    unnamed x9, local copies, waits for them, and re-layouts  11.9 us
    reduce_sum x1, other arithmetic, form_row(): return jnp.sum(lax.all_gather(piece_in, axis_name=device_axis), 0)  10.8 us
    dot_general x1, matrix products, body(): jnp.dot(ptdf_rows, load_share, preferred_element_type=jnp.float32, precis...  10.8 us
    all_gather x1, waiting for transfers between devices, body(): everyone = lax.all_gather(unit_blocks, LINE, axis=0, tiled=True)  10.1 us
  transfers between devices with their start and end apart: 3, of which 2 were waited for; matrix products, arithmetic and copies ran while one was open for 43% of the time, Pallas kernels for 0%

profile of v1, /device:TPU:1, one launch (start us, length us, event | category | flops | bytes accessed | tf_op | source)
XLA Modules:
  0.0 264.6 jit_solution(300140139826508860)
XLA Ops:
  7.2 0.0 copy-start
  7.2 0.0 all-gather.7.cloned.1.call-start
  7.2 1.5 fusion.22
  16.3 1.5 fusion.20
  28.0 2.0 broadcast_select_fusion.3
  30.0 1.0 maximum_bitcast_fusion
  31.0 0.0 all-gather.7.cloned.1.call-update
  31.1 0.7 compare_select_fusion.25
  31.8 0.7 compare_select_fusion.24
  32.5 0.7 compare_convert_fusion.23
  33.1 5.9 %multiply_add_fusion = f32[20,2048]{1,0:T(8,128)S(1)} fusion(f32[20,2048]{1,0:T(8,128)} %param.13, f32[20]{0:T(128)S(1)} %get-tuple-element.133, f32[20]{0:T(128)S(1)} %get-tuple-element.134, f32[20]{0:T(128)S(1)} %get-tuple-element.112, f32[20]{0:T(128)S(1)} %get-tuple-element.113, f32[20]{0:T(128)S(1)} %get-tuple-element.114, ...), kind=kLoop, calls=%fused_computation.17 | loop fusion | flops 3973120 | bytes 331520 | tf_op jit(solution)/shard_map/add | solution.py:50
  39.0 0.1 all_to_all.14
  39.1 0.7 copy.25
  39.9 4.8 %all-to-all-start = ((f32[20,4,512]{2,0,1:T(8,128)}), f32[20,4,512]{2,0,1:T(8,128)S(1)}, u32[]{:S(2)}, u32[]{:S(2)}) async-start(f32[20,4,512]{2,0,1:T(8,128)} %copy.25), calls=%async_computation | async-start | bytes 393216 | tf_op jit(solution)/shard_map/all_to_all | solution.py:51
  44.7 0.0 all-gather.5.cloned.1.call-start
  44.7 0.9 reshape.180
  45.6 0.1 copy.21
  45.7 0.2 reshape.182
  45.9 0.2 reshape.181
  46.0 11.9 %copy.23 = f32[128,20480]{0,1:T(8,128)} copy(f32[128,20480]{1,0:T(8,128)} %param.12) | data formatting | bytes 20971520 | tf_op args[0]
  57.9 21.9 %gather_fusion = f32[5120,128]{1,0:T(8,128)} fusion(f32[128,20480]{0,1:T(8,128)} %copy.23, s32[5120]{0:T(1024)S(1)} %broadcast_clamp_fusion), kind=kCustom, calls=%fused_computation | custom fusion | bytes 5263360 | tf_op jit(solution)/shard_map/jit(_take)/gather | solution.py:55
  79.8 4.2 %select_bitcast_fusion.1 = f32[128,5120]{0,1:T(8,128)S(1)} fusion(f32[5120,128]{1,0:T(8,128)} %gather_fusion, pred[5120]{0:T(1024)(128)(4,1)S(1)} %compare_and_fusion), kind=kLoop, calls=%fused_computation.7 | loop fusion | flops 655360 | bytes 5248000 | tf_op jit(solution)/shard_map/jit(_take)/select_n | solution.py:55
  84.0 0.0 copy-done
  84.0 0.0 copy-start.1
  84.0 0.0 copy-start.3
  84.1 10.8 %convolution_bitcast_fusion.1 = f32[128]{0:T(128)S(1)} fusion(f32[128,20480]{1,0:T(8,128)} %param.12, f32[20480,1]{0,1:T(1,128)S(1)} %bitcast.64), kind=kOutput, calls=%fused_computation.9 | convolution fusion | flops 31457280 | bytes 10568192 | tf_op jit(solution)/shard_map/dot_general | solution.py:57
  94.9 0.0 copy-done.1
  94.9 0.7 constant_dynamic-slice_fusion.36
  110.4 0.0 copy-done.3
  110.4 0.7 fusion.19
  111.1 0.0 all-to-all-done
  111.1 0.7 all_to_all.17
  111.8 0.0 all-gather.5.cloned.1.call-update
  111.8 33.6 %all-gather.7.cloned.1.call-done = f32[64,4,20480]{2,1,0:T(4,128)} async-done(((f32[1,4,20480]{2,1,0:T(4,128)}), f32[64,4,20480]{2,1,0:T(4,128)}) %all-gather.7.cloned.1.call-update) | async-done | bytes 20971536 | tf_op jit(solution)/shard_map/all_gather | solution.py:15
  145.4 10.8 %reduce_sum.9 = f32[4,20480]{1,0:T(4,128)S(1)} reduce(f32[64,4,20480]{2,1,0:T(4,128)} %all-gather.7.cloned.1.call-done, f32[]{:T(128)} %constant.115.clone.1), dimensions={0}, to_apply=%region_0.1 | reduce | flops 5160960 | bytes 21299204 | tf_op jit(solution)/shard_map/reduce_sum | solution.py:15
  156.2 0.1 fusion.18
  156.3 5.6 %copy.24 = f32[4,20480]{0,1:T(8,128)} copy(f32[4,20480]{1,0:T(4,128)S(1)} %reduce_sum.9) | data formatting | bytes 655360 | tf_op jit(solution)/shard_map/reduce_sum | solution.py:15
  161.9 0.6 constant_dynamic-slice_fusion.32
  165.1 0.6 constant_dynamic-slice_fusion.26
  167.0 0.2 multiply_subtract_fusion.2
  167.2 0.6 constant_dynamic-slice_fusion.24
  170.4 0.7 constant_dynamic-slice_fusion.10
  172.3 0.7 constant_dynamic-slice_fusion.16
  175.7 0.2 multiply_subtract_fusion.1
  175.9 0.6 constant_dynamic-slice_fusion
  179.2 0.7 constant_dynamic-slice_fusion.4
  182.3 0.7 constant_dynamic-slice_fusion.8
  186.7 0.2 multiply_subtract_fusion
  187.0 0.6 constant_dynamic-slice_fusion.12
  190.2 21.7 %gather_fusion.1 = f32[5120,4]{1,0:T(8,128)} fusion(f32[4,20480]{0,1:T(8,128)} %copy.24, s32[5120]{0:T(1024)S(1)} %broadcast_clamp_fusion), kind=kCustom, calls=%fused_computation.1 | custom fusion | bytes 184320 | tf_op jit(solution)/shard_map/jit(_take)/gather | solution.py:55
  211.9 0.6 constant_dynamic-slice_fusion.30
  212.5 1.1 multiply_subtract_fusion.4
  213.6 1.5 convolution_bitcast_fusion
  215.1 5.3 %select_bitcast_fusion = f32[4,5120]{0,1:T(8,128)} fusion(f32[5120,4]{1,0:T(8,128)} %gather_fusion.1, pred[5120]{0:T(1024)(128)(4,1)S(1)} %compare_and_fusion), kind=kLoop, calls=%fused_computation.6 | loop fusion | flops 20480 | bytes 168960 | tf_op jit(solution)/shard_map/jit(_take)/select_n | solution.py:55
  220.4 0.1 broadcast_multiply_fusion.1
  220.5 1.0 pad_maximum_fusion
  221.5 0.0 copy-start.2
  221.5 10.1 %all-gather.5.cloned.1.call-done = f32[5120,512]{1,0:T(8,128)} async-done(((f32[80,512]{1,0:T(8,128)}), f32[5120,512]{1,0:T(8,128)}) %all-gather.5.cloned.1.call-update) | async-done | bytes 10485776 | tf_op jit(solution)/shard_map/all_gather | solution.py:52
  231.7 20.4 %fusion = f32[132,512]{1,0:T(8,128)S(1)} fusion(f32[5120,512]{1,0:T(8,128)} %all-gather.5.cloned.1.call-done, f32[4,5120]{0,1:T(8,128)} %select_bitcast_fusion, f32[128,5120]{0,1:T(8,128)S(1)} %select_bitcast_fusion.1), kind=kOutput, calls=%fused_computation.2 | convolution fusion | flops 4153036800 | bytes 13459456 | tf_op jit(solution)/shard_map/dot_general | solution.py:99
  252.0 0.0 copy-done.2
  252.1 0.1 slice_subtract_fusion.1
  255.7 1.2 fusion.8
  256.9 0.9 fusion.7
  (4 shorter events, 0.1 us)
Async XLA Ops:
  7.2 76.9 %copy-start = (f32[20480]{0:T(1024)S(1)}, f32[20480]{0:T(1024)}, u32[]{:S(2)}) copy-start(f32[20480]{0:T(1024)} %param.17) | copy-start | bytes 245764
  7.2 138.2 %all-gather.7.cloned.1.call-start = ((), (), s32[]{:S(2)}) async-start(), calls=%async_computation.2 | async-start | bytes 21299200 | tf_op jit(solution)/shard_map/all_gather | solution.py:15
  39.9 71.2 %all-to-all-start = ((f32[20,4,512]{2,0,1:T(8,128)}), f32[20,4,512]{2,0,1:T(8,128)S(1)}, u32[]{:S(2)}, u32[]{:S(2)}) async-start(f32[20,4,512]{2,0,1:T(8,128)} %copy.25), calls=%async_computation | async-start | bytes 393216 | tf_op jit(solution)/shard_map/all_to_all | solution.py:51
  44.7 187.0 %all-gather.5.cloned.1.call-start = ((), (), s32[]{:S(2)}) async-start(), calls=%async_computation.1 | async-start | bytes 10649600 | tf_op jit(solution)/shard_map/all_gather | solution.py:52
  84.0 10.8 %copy-start.1 = (s32[4,2]{0,1:T(2,128)S(1)}, s32[4,2]{0,1:T(2,128)}, u32[]{:S(2)}) copy-start(s32[4,2]{0,1:T(2,128)} %param.20) | copy-start | bytes 100
  84.0 26.3 %copy-start.3 = (f32[4]{0:T(128)S(1)}, f32[4]{0:T(128)}, u32[]{:S(2)}) copy-start(f32[4]{0:T(128)} %param.23) | copy-start | bytes 52
  221.5 30.5 %copy-start.2 = (f32[512]{0:T(512)S(1)}, f32[512]{0:T(512)}, u32[]{:S(2)}) copy-start(f32[512]{0:T(512)} %param.18) | copy-start | bytes 6148
Sparse Core Ops, SparseCore 0:
  31.2 114.1 all-gather.6
  148.7 82.9 all-gather.4
